TPU v7x, 256 devices: a whole 4x4x8 slice. The times are simulated.
256 devices in a mesh: seq: 64 (over x, z, core), batch: 4 (over y).
Axes of the slice: x: 4, y: 4, z: 8, core: 2. Of those that a mesh axis runs over, the one named last changes fastest.
Arguments:
- token_ids: int32 [4, 16384], P('batch', 'seq'), may hold values from 0 to 15
- input_table: bfloat16 [16, 3840], replicated, may hold values from -6 to 6
- gate_table: bfloat16 [16, 3584], replicated, may hold values from -6 to 6
- step_table: float32 [16, 56], replicated, may hold values from -4.5 to -1.5
- decay_log: float32 [56], replicated, may hold values from -12 to 0
- conv_weight: float32 [4, 3840], replicated, may hold values from -3 to 3
- conv_bias: float32 [3840], replicated, may hold values from -3 to 3
- skip_gain: float32 [56], replicated, may hold values from 0.25 to 1.75
- norm_gain: float32 [3584], replicated, may hold values from 0.5 to 1.5
- cotangent: bfloat16 [4, 16384, 3584], P('batch', 'seq'), may hold values from -1 to 1
Outputs:
- layer_out: bfloat16 [4, 16384, 3584], P('batch', 'seq')
- input_grad: float32 [16, 3840], replicated
- gate_grad: float32 [16, 3584], replicated
- step_grad: float32 [16, 56], replicated
- decay_grad: float32 [56], replicated
- conv_weight_grad: float32 [4, 3840], replicated
- conv_bias_grad: float32 [3840], replicated
- skip_grad: float32 [56], replicated
- norm_grad: float32 [3584], replicated
All inputs are finite; a program needn't handle non-finite values.
Results may differ from a plain program's by a relative error of at most 0.014.
Values sent between devices are 32-bit elements; how exact they have to be, the bound alone decides.
No kernel may reach another device: no remote copies, remote signals or barrier semaphores. Data moves between devices by JAX's collectives and lax.ppermute only.
A program may use at most 320 MiB of HBM per device.

v0:
```python
from functools import partial

import jax
import jax.numpy as jnp
from jax import lax
from jax.sharding import PartitionSpec as P

BLOCK = 128


EPS = 1e-05
HIGH = lax.Precision.HIGHEST


def shifted(value, axis, steps):
    count = lax.axis_size(axis)
    leading, last = (max(0, -steps), min(count, count - steps))
    return lax.ppermute(value, axis, [(source, source + steps) for source in range(leading, last)])


def indicator(labels, vocab, kind):
    return (labels[:, None] == jnp.arange(vocab, dtype=jnp.int32)[None, :]).astype(kind)


def prepare(raw_rows, step_rows, decay_log, conv_weight, conv_bias, inner, heads):
    width = conv_weight.shape[0]
    tokens = raw_rows.shape[0] - width + 1
    state = (raw_rows.shape[1] - inner) // 2
    convolved = conv_bias[None, :] + conv_weight[0][None, :] * raw_rows[0:tokens]
    for offset in range(1, width):
        convolved = convolved + conv_weight[offset][None, :] * raw_rows[offset : offset + tokens]
    active = jax.nn.silu(convolved)
    values = active[:, :inner].astype(jnp.bfloat16).reshape(tokens, heads, inner // heads)
    write_keys = active[:, inner : inner + state].astype(jnp.bfloat16)
    read_keys = active[:, inner + state :].astype(jnp.bfloat16)
    steps = jax.nn.softplus(step_rows)
    log_decay = -jnp.exp(decay_log)[None, :] * steps
    return (values, write_keys, read_keys, steps, log_decay)


def group_states(values, write_keys, steps, log_decay):
    tokens, heads, head = values.shape
    count = tokens // BLOCK
    cum = jnp.cumsum(log_decay.reshape(count, BLOCK, heads), axis=1)
    factor = jnp.exp(cum[:, -1:, :] - cum) * steps.reshape(count, BLOCK, heads)
    weighted = (values.reshape(count, BLOCK, heads, head) * factor[..., None]).astype(jnp.bfloat16)
    return jnp.einsum(
        "cshp,csn->chpn",
        weighted,
        write_keys.reshape(count, BLOCK, -1),
        preferred_element_type=jnp.float32,
    )


def local_states(pieces, log_decay):
    count = pieces.shape[0]
    block_total = jnp.sum(log_decay.reshape(count, BLOCK, -1), axis=1)

    def advance(carried, item):
        piece, total = item
        return (jnp.exp(total)[:, None, None] * carried + piece, carried)

    final, entering = lax.scan(advance, jnp.zeros_like(pieces[0]), (pieces, block_total))
    return (entering, final, jnp.sum(block_total, axis=0))


def mixer_output(
    values,
    write_keys,
    read_keys,
    steps,
    log_decay,
    entering,
    carried,
    gate_rows,
    skip_gain,
    norm_gain,
):
    tokens, heads, head = values.shape
    count = tokens // BLOCK
    cum = jnp.cumsum(log_decay.reshape(count, BLOCK, heads), axis=1)
    block_total = cum[:, -1, :]
    before = jnp.cumsum(block_total, axis=0) - block_total
    states = entering + jnp.exp(before)[:, :, None, None] * carried[None]
    writes = write_keys.reshape(count, BLOCK, -1)
    reads = read_keys.reshape(count, BLOCK, -1)
    scores = jnp.einsum("ctn,csn->cts", reads, writes, preferred_element_type=jnp.float32)
    lower = (
        lax.broadcasted_iota(jnp.int32, (BLOCK, BLOCK), 0)
        >= lax.broadcasted_iota(jnp.int32, (BLOCK, BLOCK), 1)
    )[None, None]
    track = jnp.transpose(cum, (0, 2, 1))
    power = track[:, :, :, None] - track[:, :, None, :]
    fade = jnp.where(lower, jnp.exp(jnp.where(lower, power, 0.0)), 0.0)
    widths = jnp.transpose(steps.reshape(count, BLOCK, heads), (0, 2, 1))
    mixing = (scores[:, None] * fade * widths[:, :, None, :]).astype(jnp.bfloat16)
    blocked = values.reshape(count, BLOCK, heads, head)
    within = jnp.einsum("chts,cshp->cthp", mixing, blocked, preferred_element_type=jnp.float32)
    across = jnp.exp(cum)[..., None] * jnp.einsum(
        "ctn,chpn->cthp", reads, states.astype(jnp.bfloat16), preferred_element_type=jnp.float32
    )
    mixed = within + across + skip_gain[None, None, :, None] * blocked
    gated = mixed.reshape(tokens, heads * head) * jax.nn.silu(gate_rows)
    scale = lax.rsqrt(jnp.mean(gated * gated, axis=1, keepdims=True) + EPS)
    return (gated * scale * norm_gain[None, :]).astype(jnp.bfloat16)


def carry_weights(logs, backward):
    parts = logs.shape[1]
    inclusive = jnp.cumsum(logs, axis=1)
    exclusive = inclusive - logs
    rows = lax.broadcasted_iota(jnp.int32, (parts, parts), 0)
    cols = lax.broadcasted_iota(jnp.int32, (parts, parts), 1)
    if backward:
        keep = (cols > rows)[None]
        power = exclusive[:, None, :] - inclusive[:, :, None]
    else:
        keep = (cols < rows)[None]
        power = exclusive[:, :, None] - inclusive[:, None, :]
    return jnp.where(keep, jnp.exp(jnp.where(keep, power, 0.0)), 0.0)


def settle_forward(pieces):
    states_in, totals_in = pieces
    weights = carry_weights(totals_in[:, :, 0], False)
    settled = jnp.einsum("hij,hjw->hiw", weights, states_in, precision=HIGH)
    return lax.all_to_all(settled, "seq", split_axis=1, concat_axis=1, tiled=True)


def settle_backward(pieces):
    states_in, totals_in = pieces
    weights = carry_weights(totals_in[:, :, 0], True)
    settled = jnp.einsum("hij,hjw->hiw", weights, states_in, precision=HIGH)
    return lax.all_to_all(settled, "seq", split_axis=1, concat_axis=1, tiled=True)


def local(
    token_ids,
    input_table,
    gate_table,
    step_table,
    decay_log,
    conv_weight,
    conv_bias,
    skip_gain,
    norm_gain,
    cotangent,
):
    labels = token_ids[0]
    tokens = labels.shape[0]
    width = conv_weight.shape[0]
    vocab = input_table.shape[0]
    inner = gate_table.shape[1]
    heads = step_table.shape[1]
    rim = shifted(labels[tokens - width + 1 :] + 1, "seq", 1) - 1
    extended = jnp.concatenate([rim, labels])
    wide_hot = indicator(extended, vocab, jnp.bfloat16)
    own_hot = wide_hot[width - 1 :]
    raw_rows = jnp.dot(wide_hot, input_table, preferred_element_type=jnp.float32)
    gate_rows = jnp.dot(own_hot, gate_table, preferred_element_type=jnp.float32)
    step_rows = jnp.dot(own_hot.astype(jnp.float32), step_table, precision=HIGH)
    features, pull_prepare = jax.vjp(
        partial(prepare, inner=inner, heads=heads),
        raw_rows,
        step_rows,
        decay_log,
        conv_weight,
        conv_bias,
    )
    values, write_keys, read_keys, steps, log_decay = features
    pieces, pull_groups = jax.vjp(group_states, values, write_keys, steps, log_decay)
    (entering, final, total), pull_local = jax.vjp(local_states, pieces, log_decay)
    flat = final.reshape(heads, -1)
    parts = lax.axis_size("seq")
    span = flat.shape[1] // parts
    totals = jnp.broadcast_to(total[:, None, None], (heads, parts, 1))
    carried = settle_forward(
        (
            lax.all_to_all(
                flat.reshape(heads, parts, span), "seq", split_axis=1, concat_axis=1, tiled=True
            ),
            lax.all_to_all(totals, "seq", split_axis=1, concat_axis=1, tiled=True),
        )
    )
    layer_out, pull_out = jax.vjp(
        mixer_output,
        values,
        write_keys,
        read_keys,
        steps,
        log_decay,
        entering,
        carried,
        gate_rows,
        skip_gain,
        norm_gain,
    )
    d_values, d_write, d_read, d_steps, d_log, d_entering, d_carried, d_gate, d_skip, d_norm = (
        pull_out(cotangent[0])
    )
    back_flat = d_carried.reshape(heads, -1)
    later = settle_backward(
        (
            lax.all_to_all(
                back_flat.reshape(heads, parts, span),
                "seq",
                split_axis=1,
                concat_axis=1,
                tiled=True,
            ),
            lax.all_to_all(totals, "seq", split_axis=1, concat_axis=1, tiled=True),
        )
    )
    d_total = jnp.exp(total) * jnp.sum(later * carried, axis=(1, 2))
    d_pieces, d_log_local = pull_local((d_entering, later, d_total))
    d_values_state, d_write_state, d_steps_state, d_log_state = pull_groups(d_pieces)
    d_raw, d_step_rows, d_decay, d_taps, d_shift = pull_prepare(
        (
            d_values + d_values_state,
            d_write + d_write_state,
            d_read,
            d_steps + d_steps_state,
            d_log + d_log_state + d_log_local,
        )
    )
    wide_float = wide_hot.astype(jnp.float32)
    own_float = wide_float[width - 1 :]
    sums = lax.psum(
        (
            jnp.dot(wide_float.T, d_raw, precision=HIGH),
            jnp.dot(own_float.T, d_gate, precision=HIGH),
            jnp.dot(own_float.T, d_step_rows, precision=HIGH),
            d_decay,
            d_taps,
            d_shift,
            d_skip,
            d_norm,
        ),
        ("seq", "batch"),
    )
    return (layer_out[None], sums[0], sums[1], sums[2], sums[3], sums[4], sums[5], sums[6], sums[7])


def solution(mesh):
    return jax.shard_map(
        local,
        mesh=mesh,
        in_specs=(
            P("batch", "seq"),
            P(),
            P(),
            P(),
            P(),
            P(),
            P(),
            P(),
            P(),
            P("batch", "seq", None),
        ),
        out_specs=(P("batch", "seq", None), P(), P(), P(), P(), P(), P(), P(), P()),
        check_vma=False,
    )
```

profile of v0, /device:TPU:1, one launch (start us, length us, event | category | flops | bytes accessed | tf_op | source)
XLA Modules:
  0.0 922.5 jit_solution(5737111355359867479)
XLA Ops:
  8.0 4.9 collective-permute-start
  16.4 3.9 multiply_convert_fusion.1
  24.3 12.3 %all-to-all-start = ((f32[56,64,1]{0,2,1:T(1,128)}), f32[56,64,1]{0,2,1:T(1,128)S(1)}, u32[]{:S(2)}, u32[]{:S(2)}) async-start(f32[56,64,1]{0,2,1:T(1,128)} %broadcast_in_dim.130), calls=%async_computation | async-start | bytes 65536 | tf_op jit(solution)/shard_map/all_to_all | solution.py:182
  37.3 5.6 reshape.281
  42.9 6.4 copy.258
  49.3 3.9 fusion.81
  53.2 6.2 while.38
  59.4 2.3 copy.267
  61.7 10.7 %all-to-all-start.1 = ((f32[56,64,128]{2,0,1:T(8,128)}), f32[56,64,128]{2,0,1:T(8,128)S(1)}, u32[]{:S(2)}, u32[]{:S(2)}) async-start(f32[56,64,128]{2,0,1:T(8,128)} %copy.267), calls=%async_computation.1 | async-start | bytes 3670016 | tf_op jit(solution)/shard_map/all_to_all | solution.py:179
  72.8 45.0 %all-to-all-done.1 = f32[56,64,128]{2,0,1:T(8,128)S(1)} async-done(((f32[56,64,128]{2,0,1:T(8,128)}), f32[56,64,128]{2,0,1:T(8,128)S(1)}, u32[]{:S(2)}, u32[]{:S(2)}) %all-to-all-start.1) | async-done | bytes 1835040 | tf_op jit(solution)/shard_map/all_to_all | solution.py:179
  117.7 2.4 fusion.60
  120.1 2.3 copy.269
  122.4 6.0 all-to-all-start.2
  128.7 45.0 %all-to-all-done.2 = f32[56,64,128]{2,0,1:T(8,128)S(1)} async-done(((f32[56,64,128]{2,0,1:T(8,128)}), f32[56,64,128]{2,0,1:T(8,128)S(1)}, u32[]{:S(2)}, u32[]{:S(2)}) %all-to-all-start.2) | async-done | bytes 1835040 | tf_op jit(solution)/shard_map/all_to_all | solution.py:127
  174.1 3.0 copy-done.6
  181.4 5.5 fusion.31
  186.8 8.9 copy.308
  195.7 6.9 reshape.282
  202.6 3.5 multiply_reduce_fusion.8
  209.2 3.9 multiply_reduce_fusion.4
  213.1 5.1 copy.273
  218.3 5.5 reshape.269
  223.8 4.6 multiply_reduce_fusion.5
  228.4 2.3 copy.278
  230.7 16.6 %all-to-all-start.3 = ((f32[56,64,128]{2,0,1:T(8,128)}), f32[56,64,128]{2,0,1:T(8,128)S(1)}, u32[]{:S(2)}, u32[]{:S(2)}) async-start(f32[56,64,128]{2,0,1:T(8,128)} %copy.278), calls=%async_computation.3 | async-start | bytes 3670016 | tf_op jit(solution)/shard_map/all_to_all | solution.py:204
  249.2 43.6 %all-to-all-done.3 = f32[56,64,128]{2,0,1:T(8,128)S(1)} async-done(((f32[56,64,128]{2,0,1:T(8,128)}), f32[56,64,128]{2,0,1:T(8,128)S(1)}, u32[]{:S(2)}, u32[]{:S(2)}) %all-to-all-start.3) | async-done | bytes 1835040 | tf_op jit(solution)/shard_map/all_to_all | solution.py:204
  292.8 2.4 fusion.58
  295.2 2.3 copy.280
  297.5 6.2 all-to-all-start.4
  303.7 8.6 fusion.14
  312.6 3.9 multiply_reduce_fusion.6
  316.7 3.9 convert_element_type.99
  323.6 3.0 fusion.95
  327.2 6.4 fusion.35
  333.5 15.5 %all-to-all-done.4 = f32[56,64,128]{2,0,1:T(8,128)} async-done(((f32[56,64,128]{2,0,1:T(8,128)}), f32[56,64,128]{2,0,1:T(8,128)}, u32[]{:S(2)}, u32[]{:S(2)}) %all-to-all-start.4) | async-done | bytes 1835040 | tf_op jit(solution)/shard_map/all_to_all | solution.py:134
  350.9 9.6 %while.37 = (s32[]{:T(128)}, f32[56,64,128]{2,1,0:T(8,128)S(1)}, bf16[2,56,64,128]{3,2,1,0:T(8,128)(2,1)}, f32[2,56]{1,0:T(2,128)S(1)}, f32[2,56,64,128]{3,2,1,0...) while((s32[]{:T(128)}, f32[56,64,128]{2,1,0:T(8,128)S(1)}, ...), condition=%wide.region_13.14_spmd.clone, body=%wide.region_11.13_spmd.sunk.clone | while | flops 1835011 | bytes 25692272 | solution.py:63
  353.3 2.3 fusion.180
  358.0 2.3 fusion.180
  360.5 3.0 fusion.92
  367.4 4.2 fusion.57
  371.8 2.2 reduce_window_sum.74
  375.7 6.6 copy.303
  382.4 4.8 reshape.280
  387.1 9.8 %multiply_reduce_fusion.3 = (f32[3840]{0:T(1024)S(1)}, f32[3840]{0:T(1024)S(1)}, f32[3840]{0:T(1024)S(1)}, f32[3840]{0:T(1024)S(1)}, f32[3840]{0:T(1024)}, /*index=5*/f32[256,3840]{1,0:T(8,128)S(1)}) fusion(f32[259,3840]{1,0:T(8,128)} %copy-done.2, f32[256,3840]{1,0:T(8,128)} %get-tuple-element.382, bf16[256,3584]{1,0:T(8,128)(2,1)S(1)} %reshape.280, ...), kind=kLoop, calls=%fused_computation.52 | loop fusion | flops 22590720 | bytes 25635840 | tf_op jit(solution)/shard_map/transpose(jvp())/reduce_sum | solution.py:31
  397.0 5.8 broadcast_multiply_fusion
  403.6 8.9 fusion.17
  412.5 235.1 %all-reduce.18.cloned.1.call-done = (f32[16,56]{1,0:T(8,128)}, f32[56]{0:T(128)}, f32[4,3840]{1,0:T(4,128)}, f32[3840]{0:T(1024)}, f32[56]{0:T(128)}, /*index=5*/f32[3584]{0:T(1024)}) async-done(((f32[16,56]{1,0:T(8,128)}, f32[56]{0:T(128)}, f32[4,3840]{1,0:T(4,128)}, f32[3840]{0:T(1024)}, f32[56]{0:T(128)}, /*index=5*/f32[3584]{0:T(1024)}), (f32[16,56]{1,0:T(8,128)}, f32[56]{0:T(128)}, ...) | async-done | bytes 95184 | tf_op jit(solution)/shard_map/psum | solution.py:228
  647.6 256.7 %all-reduce.20.cloned.1.call-done = (f32[16,3840]{1,0:T(8,128)}, f32[16,3584]{1,0:T(8,128)}) async-done(((f32[16,3840]{1,0:T(8,128)}, f32[16,3584]{1,0:T(8,128)}), (f32[16,3840]{1,0:T(8,128)}, f32[16,3584]{1,0:T(8,128)})) %all-reduce.20.cloned.1.call-update) | async-done | bytes 475152 | tf_op jit(solution)/shard_map/psum | solution.py:228
  (190 shorter events, 53.3 us)
Async XLA Ops:
  7.2 8.4 copy-start
  8.0 6.8 collective-permute-start
  13.6 9.3 %copy-start.38 = (f32[56]{0:T(128)}, f32[56]{0:T(128)S(1)}, u32[]{:S(2)}) copy-start(f32[56]{0:T(128)S(1)} %exponential_negate_fusion) | copy-start | bytes 676
  16.4 3.9 copy-start.2
  20.3 1.3 copy-start.7
  20.3 2.6 copy-start.32
  23.3 19.6 %copy-start.29 = (f32[56]{0:T(128)}, f32[56]{0:T(128)S(1)}, u32[]{:S(2)}) copy-start(f32[56]{0:T(128)S(1)} %get-tuple-element.379) | copy-start | bytes 676
  24.3 37.4 %all-to-all-start = ((f32[56,64,1]{0,2,1:T(1,128)}), f32[56,64,1]{0,2,1:T(1,128)S(1)}, u32[]{:S(2)}, u32[]{:S(2)}) async-start(f32[56,64,1]{0,2,1:T(1,128)} %broadcast_in_dim.130), calls=%async_computation | async-start | bytes 65536 | tf_op jit(solution)/shard_map/all_to_all | solution.py:182
  53.2 2.7 copy-start.4
  56.4 2.7 copy-start.4
  59.4 2.3 copy-start.33
  61.7 56.0 %all-to-all-start.1 = ((f32[56,64,128]{2,0,1:T(8,128)}), f32[56,64,128]{2,0,1:T(8,128)S(1)}, u32[]{:S(2)}, u32[]{:S(2)}) async-start(f32[56,64,128]{2,0,1:T(8,128)} %copy.267), calls=%async_computation.1 | async-start | bytes 3670016 | tf_op jit(solution)/shard_map/all_to_all | solution.py:179
  122.4 51.4 %all-to-all-start.2 = ((f32[56,64,128]{2,0,1:T(8,128)}), f32[56,64,128]{2,0,1:T(8,128)S(1)}, u32[]{:S(2)}, u32[]{:S(2)}) async-start(f32[56,64,128]{2,0,1:T(8,128)} %copy.269), calls=%async_computation.2 | async-start | bytes 3670016 | tf_op jit(solution)/shard_map/all_to_all | solution.py:127
  128.4 175.3 %copy-start.27 = (pred[128,128]{1,0:T(8,128)(4,1)}, pred[128,128]{1,0:T(8,128)(4,1)S(1)}, u32[]{:S(2)}) copy-start(pred[128,128]{1,0:T(8,128)(4,1)S(1)} %iota_compare_fusion.3) | copy-start | bytes 49156
  173.8 3.9 copy-start.9
  173.8 3.4 copy-start.6
  174.1 3.5 copy-start.14
  177.6 3.7 copy-start.11
  177.6 3.7 copy-start.35
  179.5 1.8 copy-start.20
  195.7 6.9 copy-start.31
  202.6 3.6 copy-start.21
  202.6 3.6 copy-start.25
  206.2 7.0 copy-start.18
  206.2 7.0 copy-start.24
  206.2 3.0 copy-start.8
  218.3 5.5 copy-start.15
  230.7 62.1 %all-to-all-start.3 = ((f32[56,64,128]{2,0,1:T(8,128)}), f32[56,64,128]{2,0,1:T(8,128)S(1)}, u32[]{:S(2)}, u32[]{:S(2)}) async-start(f32[56,64,128]{2,0,1:T(8,128)} %copy.278), calls=%async_computation.3 | async-start | bytes 3670016 | tf_op jit(solution)/shard_map/all_to_all | solution.py:204
  295.2 8.6 copy-start.12
  297.5 51.5 %all-to-all-start.4 = ((f32[56,64,128]{2,0,1:T(8,128)}), f32[56,64,128]{2,0,1:T(8,128)}, u32[]{:S(2)}, u32[]{:S(2)}) async-start(f32[56,64,128]{2,0,1:T(8,128)} %copy.280), calls=%async_computation.4 | async-start | bytes 3670016 | tf_op jit(solution)/shard_map/all_to_all | solution.py:134
  303.7 343.9 %all-reduce.18.cloned.1.call-start = ((), (), s32[]{:S(2)}) async-start(), calls=%async_computation.5 | async-start | bytes 206848 | tf_op jit(solution)/shard_map/psum | solution.py:228
  316.6 7.1 copy-start.17
  323.5 3.2 copy-start.19
  323.5 3.7 copy-start.22
  333.5 17.3 %copy-start.34 = (f32[2,56,1,1]{1,3,2,0:T(1,128)S(1)}, f32[2,56,1,1]{1,3,2,0:T(1,128)}, u32[]{:S(2)}) copy-start(f32[2,56,1,1]{1,3,2,0:T(1,128)} %copy-done.33) | copy-start | bytes 1348
  350.9 2.4 copy-start.5
  355.7 2.4 copy-start.5
  360.4 3.0 copy-start.13
  360.4 3.1 copy-start.23
  363.6 1.5 copy-start.10
  363.6 3.5 copy-start.30
  363.6 3.7 copy-start.3
  363.6 3.7 copy-start.28
  363.6 3.7 copy-start.36
  367.3 6.9 copy-start.37
  367.4 7.5 copy-start.39
  403.5 500.8 %all-reduce.20.cloned.1.call-start = ((), (), s32[]{:S(2)}) async-start(), calls=%async_computation.6 | async-start | bytes 950272 | tf_op jit(solution)/shard_map/psum | solution.py:228
  403.6 511.7 %copy-start.1 = (bf16[16,3840]{1,0:T(8,128)(2,1)S(1)}, bf16[16,3840]{1,0:T(8,128)(2,1)}, u32[]{:S(2)}) copy-start(bf16[16,3840]{1,0:T(8,128)(2,1)} %param.15) | copy-start | bytes 368644
  (2 other events, 2.0 us)
Sparse Core Ops, SparseCore 0:
  403.6 243.8 all-reduce.17
  653.7 250.5 all-reduce.19
where the time goes:
time: 933 us; the launch traced here: 923 us
  waiting for transfers between devices  641 us (69%)
  local copies, waits for them, and re-layouts  94 us (10%)
  matrix products  60.2 us (6%)
  starting transfers between devices  56.7 us (6%)
  other arithmetic  55.3 us (6%)
  between operations  15.2 us (2%)
    psum x2, waiting for transfers between devices, local(): lax.psum((jnp.dot(wide_float.T, d_raw, precision=HIGH), jnp.dot(own_float...  492 us
    all_to_all x1, waiting for transfers between devices, settle_forward(): lax.all_to_all(settled, 'seq', split_axis=1, concat_axis=1, tiled=True)  45 us
    all_to_all x1, waiting for transfers between devices, local(): lax.all_to_all(flat.reshape(heads, parts, span), 'seq', split_axis=1, con...  45 us
    all_to_all x1, waiting for transfers between devices, local(): lax.all_to_all(back_flat.reshape(heads, parts, span), 'seq', split_axis=1...  43.6 us
    reshape x3, local copies, waits for them, and re-layouts, mixer_output(): gated = mixed.reshape(tokens, heads * head) * jax.nn.silu(gate_rows)  21.3 us
    unnamed x85, local copies, waits for them, and re-layouts  20.6 us
  transfers between devices with their start and end apart: 8, of which 6 were waited for; matrix products, arithmetic and copies ran while one was open for 7% of the time, Pallas kernels for 0%

commit v1 on v0

--- a/solution.py
+++ b/solution.py
@@ -225,19 +225,23 @@
     )
     wide_float = wide_hot.astype(jnp.float32)
     own_float = wide_float[width - 1 :]
-    sums = lax.psum(
-        (
-            jnp.dot(wide_float.T, d_raw, precision=HIGH),
-            jnp.dot(own_float.T, d_gate, precision=HIGH),
-            jnp.dot(own_float.T, d_step_rows, precision=HIGH),
-            d_decay,
-            d_taps,
-            d_shift,
-            d_skip,
-            d_norm,
-        ),
-        ("seq", "batch"),
-    )
+    parts_list = (
+        jnp.dot(wide_float.T, d_raw, precision=HIGH),
+        jnp.dot(own_float.T, d_gate, precision=HIGH),
+        jnp.dot(own_float.T, d_step_rows, precision=HIGH),
+        d_decay,
+        d_taps,
+        d_shift,
+        d_skip,
+        d_norm,
+    )
+    packed = jnp.concatenate([part.reshape(-1) for part in parts_list])
+    packed = lax.psum(packed, ("seq", "batch"))
+    sums = []
+    offset = 0
+    for part in parts_list:
+        sums.append(packed[offset : offset + part.size].reshape(part.shape))
+        offset += part.size
     return (layer_out[None], sums[0], sums[1], sums[2], sums[3], sums[4], sums[5], sums[6], sums[7])
 
 

time: 933 us -> 687 us (0.74)
  waiting for transfers between devices: 641 us -> 398 us
    psum x2 -> x1, waiting for transfers between devices: 492 us -> 249 us  [local(): packed = lax.psum(packed, ('seq', 'batch'))]
    unnamed x85 -> x61, local copies, waits for them, and re-layouts: 20.6 us -> 9.66 us
  transfers between devices with their start and end apart: 8 -> 7, of which waited for: 6 -> 5; matrix products, arithmetic and copies ran while one was open for 7% -> 8% of each run, Pallas kernels for 0% -> 0%
where the time goes in v1:
time: 687 us; the launch traced here: 678 us
  waiting for transfers between devices  398 us (58%)
  local copies, waits for them, and re-layouts  103 us (15%)
  starting transfers between devices  56.6 us (8%)
  matrix products  53.5 us (8%)
  other arithmetic  51.2 us (7%)
  between operations  15.2 us (2%)
    psum x1, waiting for transfers between devices, local(): packed = lax.psum(packed, ('seq', 'batch'))  249 us
    all_to_all x1, waiting for transfers between devices, settle_forward(): lax.all_to_all(settled, 'seq', split_axis=1, concat_axis=1, tiled=True)  45 us
    all_to_all x1, waiting for transfers between devices, local(): lax.all_to_all(flat.reshape(heads, parts, span), 'seq', split_axis=1, con...  45 us
    all_to_all x1, waiting for transfers between devices, local(): lax.all_to_all(back_flat.reshape(heads, parts, span), 'seq', split_axis=1...  43.7 us
    reshape x3, local copies, waits for them, and re-layouts, mixer_output(): gated = mixed.reshape(tokens, heads * head) * jax.nn.silu(gate_rows)  21.3 us
    dot_general x3, matrix products, mixer_output(): jnp.einsum('chts,cshp->cthp', mixing, blocked, preferred_element_type=jnp...  18.3 us
    all_to_all x1, starting transfers between devices, local(): lax.all_to_all(back_flat.reshape(heads, parts, span), 'seq', split_axis=1...  16.6 us
    all_to_all x1, waiting for transfers between devices, settle_backward(): lax.all_to_all(settled, 'seq', split_axis=1, concat_axis=1, tiled=True)  15.6 us
  transfers between devices with their start and end apart: 7, of which 5 were waited for; matrix products, arithmetic and copies ran while one was open for 8% of the time, Pallas kernels for 0%

profile of v1, /device:TPU:1, one launch (start us, length us, event | category | flops | bytes accessed | tf_op | source)
XLA Modules:
  0.0 678.2 jit_solution(8957550954061912077)
XLA Ops:
  8.0 4.9 collective-permute-start
  16.4 3.9 multiply_convert_fusion.1
  24.3 12.3 %all-to-all-start = ((f32[56,64,1]{0,2,1:T(1,128)}), f32[56,64,1]{0,2,1:T(1,128)S(1)}, u32[]{:S(2)}, u32[]{:S(2)}) async-start(f32[56,64,1]{0,2,1:T(1,128)} %broadcast_in_dim.130), calls=%async_computation | async-start | bytes 65536 | tf_op jit(solution)/shard_map/all_to_all | solution.py:182
  37.3 5.6 reshape.313
  42.9 6.4 copy.258
  49.3 3.9 fusion.81
  53.2 6.2 while.38
  59.4 2.3 copy.267
  61.7 10.7 %all-to-all-start.1 = ((f32[56,64,128]{2,0,1:T(8,128)}), f32[56,64,128]{2,0,1:T(8,128)S(1)}, u32[]{:S(2)}, u32[]{:S(2)}) async-start(f32[56,64,128]{2,0,1:T(8,128)} %copy.267), calls=%async_computation.1 | async-start | bytes 3670016 | tf_op jit(solution)/shard_map/all_to_all | solution.py:179
  72.7 45.0 %all-to-all-done.1 = f32[56,64,128]{2,0,1:T(8,128)S(1)} async-done(((f32[56,64,128]{2,0,1:T(8,128)}), f32[56,64,128]{2,0,1:T(8,128)S(1)}, u32[]{:S(2)}, u32[]{:S(2)}) %all-to-all-start.1) | async-done | bytes 1835040 | tf_op jit(solution)/shard_map/all_to_all | solution.py:179
  117.7 2.4 fusion.60
  120.1 2.3 copy.269
  122.4 6.0 all-to-all-start.2
  128.7 45.0 %all-to-all-done.2 = f32[56,64,128]{2,0,1:T(8,128)S(1)} async-done(((f32[56,64,128]{2,0,1:T(8,128)}), f32[56,64,128]{2,0,1:T(8,128)S(1)}, u32[]{:S(2)}, u32[]{:S(2)}) %all-to-all-start.2) | async-done | bytes 1835040 | tf_op jit(solution)/shard_map/all_to_all | solution.py:127
  174.1 3.0 copy-done.6
  181.3 5.5 fusion.31
  186.8 8.9 %copy.308 = f32[2,128,56,64]{3,2,1,0:T(8,128)} copy(f32[2,128,56,64]{1,3,2,0:T(8,128)} %fusion.31) | data formatting | bytes 7340032 | tf_op jit(solution)/shard_map/jvp()/reshape | solution.py:103
  195.7 6.9 %reshape.314 = f32[256,3584]{1,0:T(8,128)} reshape(f32[2,128,56,64]{3,2,1,0:T(8,128)} %copy.308) | data formatting | bytes 7340032 | tf_op jit(solution)/shard_map/jvp()/reshape | solution.py:103
  202.6 3.5 multiply_reduce_fusion.8
  209.2 3.9 multiply_reduce_fusion.4
  213.1 5.1 copy.273
  218.3 5.5 reshape.293
  223.8 4.5 multiply_reduce_fusion.5
  228.3 2.3 copy.278
  230.6 16.6 %all-to-all-start.3 = ((f32[56,64,128]{2,0,1:T(8,128)}), f32[56,64,128]{2,0,1:T(8,128)S(1)}, u32[]{:S(2)}, u32[]{:S(2)}) async-start(f32[56,64,128]{2,0,1:T(8,128)} %copy.278), calls=%async_computation.3 | async-start | bytes 3670016 | tf_op jit(solution)/shard_map/all_to_all | solution.py:204
  249.0 43.7 %all-to-all-done.3 = f32[56,64,128]{2,0,1:T(8,128)S(1)} async-done(((f32[56,64,128]{2,0,1:T(8,128)}), f32[56,64,128]{2,0,1:T(8,128)S(1)}, u32[]{:S(2)}, u32[]{:S(2)}) %all-to-all-start.3) | async-done | bytes 1835040 | tf_op jit(solution)/shard_map/all_to_all | solution.py:204
  292.7 2.4 fusion.58
  295.1 2.4 copy.280
  297.4 6.2 all-to-all-start.4
  303.7 6.6 fusion.35
  311.1 8.6 %fusion.14 = (f32[2,56,128]{2,1,0:T(8,128)S(1)}, f32[2,56,128]{2,1,0:T(8,128)S(1)}, f32[2,56,128]{2,1,0:T(8,128)S(1)}, bf16[2,128,128]{2,1,0:T(8,128)(2,1)S(1)}) fusion(f32[2,56,128]{2,1,0:T(8,128)S(1)} %copy.257, f32[2,56,128]{2,1,0:T(8,128)S(1)} %copy.255, f32[2,128,128]{2,1,0:T(8,128)S(1)} %fusion.152, pred[128,128]{1,0:T(8,128)(4,1)S(1)} %iota_compare_fusion.3, ...), kind=kOutput, calls=%fused_computation.28 | convolution fusion | flops 264165376 | bytes 6004736 | tf_op jit(solution)/shard_map/transpose(jvp(chts,cshp->cthp))/dot_general | solution.py:98
  320.0 3.9 multiply_reduce_fusion.6
  324.1 3.9 convert_element_type.99
  328.1 2.2 reduce_window_sum.73
  330.5 2.9 fusion.95
  333.3 15.6 %all-to-all-done.4 = f32[56,64,128]{2,0,1:T(8,128)} async-done(((f32[56,64,128]{2,0,1:T(8,128)}), f32[56,64,128]{2,0,1:T(8,128)}, u32[]{:S(2)}, u32[]{:S(2)}) %all-to-all-start.4) | async-done | bytes 1835040 | tf_op jit(solution)/shard_map/all_to_all | solution.py:134
  350.8 9.6 %while.37 = (s32[]{:T(128)}, f32[56,64,128]{2,1,0:T(8,128)S(1)}, bf16[2,56,64,128]{3,2,1,0:T(8,128)(2,1)}, f32[2,56]{1,0:T(2,128)S(1)}, f32[2,56,64,128]{3,2,1,0...) while((s32[]{:T(128)}, f32[56,64,128]{2,1,0:T(8,128)S(1)}, ...), condition=%wide.region_13.14_spmd.clone, body=%wide.region_11.13_spmd.sunk.clone | while | flops 1835011 | bytes 25692272 | solution.py:63
  353.2 2.3 fusion.181
  358.0 2.3 fusion.181
  360.4 3.0 fusion.92
  367.3 4.2 fusion.57
  374.6 6.7 copy.303
  381.3 4.8 reshape.312
  386.0 10.4 %multiply_reduce_fusion.3 = (f32[3840]{0:T(1024)S(1)}, f32[3840]{0:T(1024)S(1)}, f32[3840]{0:T(1024)S(1)}, f32[3840]{0:T(1024)S(1)}, f32[3840]{0:T(1024)S(1)}, /*index=5*/f32[256,3840]{1,0:T(8,128)}) fusion(f32[259,3840]{1,0:T(8,128)} %copy-done.2, f32[256,3840]{1,0:T(8,128)} %get-tuple-element.374, bf16[256,3584]{1,0:T(8,128)(2,1)S(1)} %reshape.312, ...), kind=kLoop, calls=%fused_computation.52 | loop fusion | flops 22590720 | bytes 25635840 | tf_op jit(solution)/shard_map/transpose(jvp())/reduce_sum | solution.py:31
  396.6 3.3 broadcast_multiply_fusion
  400.0 2.7 fusion.17
  402.7 8.7 %concatenate.7 = f32[142576]{0:T(1024)} concatenate(f32[61440]{0:T(1024)S(1)} %reshape.294, f32[57344]{0:T(1024)} %reshape.295, f32[896]{0:T(1024)S(1)} %reshape.297, f32[56]{0:T(128)S(1)} %negate_multiply_fusion, f32[15360]{0:T(1024)S(1)} %reshape.302, f32[3840]{0:T(1024)S(1)} %get-tuple-element.321, f32[56]{0:T(128)S(1)} %reduce_sum.274, f32[3584]{0:T(1024)S(1)} %get-tuple-element.319), dimensions={0} | concatenate | bytes 1140608 | tf_op jit(solution)/shard_map/concatenate | solution.py:238
  411.4 249.1 %all-reduce.15.cloned.1.call-done = f32[142576]{0:T(1024)} async-done(((f32[142576]{0:T(1024)}), f32[142576]{0:T(1024)}) %all-reduce.15.cloned.1.call-update) | async-done | bytes 570320 | tf_op jit(solution)/shard_map/psum | solution.py:239
  (179 shorter events, 50.6 us)
Async XLA Ops:
  7.2 8.4 %copy-start = (bf16[16,3840]{1,0:T(8,128)(2,1)S(1)}, bf16[16,3840]{1,0:T(8,128)(2,1)}, u32[]{:S(2)}) copy-start(bf16[16,3840]{1,0:T(8,128)(2,1)} %param.15) | copy-start | bytes 368644
  8.0 6.8 collective-permute-start
  13.6 9.3 %copy-start.30 = (f32[56]{0:T(128)}, f32[56]{0:T(128)S(1)}, u32[]{:S(2)}) copy-start(f32[56]{0:T(128)S(1)} %exponential_negate_fusion) | copy-start | bytes 676
  15.6 0.8 copy-start.24
  16.4 3.9 copy-start.2
  20.3 1.3 copy-start.7
  20.3 2.6 copy-start.26
  24.3 37.4 %all-to-all-start = ((f32[56,64,1]{0,2,1:T(1,128)}), f32[56,64,1]{0,2,1:T(1,128)S(1)}, u32[]{:S(2)}, u32[]{:S(2)}) async-start(f32[56,64,1]{0,2,1:T(1,128)} %broadcast_in_dim.130), calls=%async_computation | async-start | bytes 65536 | tf_op jit(solution)/shard_map/all_to_all | solution.py:182
  53.2 2.7 copy-start.4
  56.3 2.7 copy-start.4
  61.7 56.0 %all-to-all-start.1 = ((f32[56,64,128]{2,0,1:T(8,128)}), f32[56,64,128]{2,0,1:T(8,128)S(1)}, u32[]{:S(2)}, u32[]{:S(2)}) async-start(f32[56,64,128]{2,0,1:T(8,128)} %copy.267), calls=%async_computation.1 | async-start | bytes 3670016 | tf_op jit(solution)/shard_map/all_to_all | solution.py:179
  122.4 51.4 %all-to-all-start.2 = ((f32[56,64,128]{2,0,1:T(8,128)}), f32[56,64,128]{2,0,1:T(8,128)S(1)}, u32[]{:S(2)}, u32[]{:S(2)}) async-start(f32[56,64,128]{2,0,1:T(8,128)} %copy.269), calls=%async_computation.2 | async-start | bytes 3670016 | tf_op jit(solution)/shard_map/all_to_all | solution.py:127
  173.7 3.9 copy-start.9
  173.7 3.4 copy-start.6
  174.1 3.5 copy-start.14
  177.6 1.2 copy-start.16
  177.6 3.7 copy-start.11
  177.6 3.7 copy-start.27
  179.5 1.8 copy-start.19
  195.7 6.9 %copy-start.25 = (bf16[16,3584]{1,0:T(8,128)(2,1)S(1)}, bf16[16,3584]{1,0:T(8,128)(2,1)}, u32[]{:S(2)}) copy-start(bf16[16,3584]{1,0:T(8,128)(2,1)} %param.16) | copy-start | bytes 344068
  202.6 3.6 copy-start.20
  202.6 3.6 copy-start.23
  206.2 7.0 %copy-start.18 = (f32[256,3584]{1,0:T(8,128)}, f32[256,3584]{1,0:T(8,128)S(1)}, u32[]{:S(2)}) copy-start(f32[256,3584]{1,0:T(8,128)S(1)} %get-tuple-element.370) | copy-start | bytes 11010052
  206.2 7.0 %copy-start.22 = (f32[256,3584]{1,0:T(8,128)}, f32[256,3584]{1,0:T(8,128)S(1)}, u32[]{:S(2)}) copy-start(f32[256,3584]{1,0:T(8,128)S(1)} %get-tuple-element.389) | copy-start | bytes 11010052
  206.2 3.0 copy-start.8
  218.3 5.5 copy-start.15
  230.6 62.0 %all-to-all-start.3 = ((f32[56,64,128]{2,0,1:T(8,128)}), f32[56,64,128]{2,0,1:T(8,128)S(1)}, u32[]{:S(2)}, u32[]{:S(2)}) async-start(f32[56,64,128]{2,0,1:T(8,128)} %copy.278), calls=%async_computation.3 | async-start | bytes 3670016 | tf_op jit(solution)/shard_map/all_to_all | solution.py:204
  297.4 51.5 %all-to-all-start.4 = ((f32[56,64,128]{2,0,1:T(8,128)}), f32[56,64,128]{2,0,1:T(8,128)}, u32[]{:S(2)}, u32[]{:S(2)}) async-start(f32[56,64,128]{2,0,1:T(8,128)} %copy.280), calls=%async_computation.4 | async-start | bytes 3670016 | tf_op jit(solution)/shard_map/all_to_all | solution.py:134
  303.6 7.5 %copy-start.12 = (bf16[2,128,56,64]{1,3,2,0:T(8,128)(2,1)S(1)}, bf16[2,128,56,64]{1,3,2,0:T(8,128)(2,1)}, u32[]{:S(2)}) copy-start(bf16[2,128,56,64]{1,3,2,0:T(8,128)(2,1)} %copy.258) | copy-start | bytes 5505028
  303.6 356.9 %all-reduce.15.cloned.1.call-start = ((), (), s32[]{:S(2)}) async-start(), calls=%async_computation.5 | async-start | bytes 1146880 | tf_op jit(solution)/shard_map/psum | solution.py:239
  323.9 6.5 copy-start.17
  350.8 2.4 copy-start.5
  355.6 2.4 copy-start.5
  360.4 3.0 copy-start.13
  360.4 3.1 copy-start.21
  363.5 1.5 copy-start.10
  363.5 3.7 copy-start.3
  363.5 3.7 copy-start.28
  367.2 6.9 %copy-start.29 = (f32[56]{0:T(128)S(1)}, f32[56]{0:T(128)}, u32[]{:S(2)}) copy-start(f32[56]{0:T(128)} %param.18) | copy-start | bytes 676
  367.3 7.0 %copy-start.31 = (f32[56]{0:T(128)S(1)}, f32[56]{0:T(128)}, u32[]{:S(2)}) copy-start(f32[56]{0:T(128)} %copy-done.30) | copy-start | bytes 676
  400.0 271.0 %copy-start.1 = (bf16[16,3840]{1,0:T(8,128)(2,1)S(1)}, bf16[16,3840]{1,0:T(8,128)(2,1)}, u32[]{:S(2)}) copy-start(bf16[16,3840]{1,0:T(8,128)(2,1)} %param.15) | copy-start | bytes 368644
Sparse Core Ops, SparseCore 0:
  411.6 248.9 all-reduce.14

commit v2 on v1

--- a/solution.py
+++ b/solution.py
@@ -134,6 +134,20 @@
     return lax.all_to_all(settled, "seq", split_axis=1, concat_axis=1, tiled=True)
 
 
+def spread_sum(flat, axes):
+    count = 1
+    for axis in axes:
+        count *= lax.axis_size(axis)
+    size = flat.shape[0]
+    chunk = -(-size // count)
+    padded = jnp.pad(flat, (0, chunk * count - size)).reshape(count, chunk)
+    gathered = lax.all_to_all(padded, axes, split_axis=0, concat_axis=0, tiled=True)
+    reduced = jnp.sum(gathered, axis=0, keepdims=True)
+    spread = jnp.broadcast_to(reduced, (count, chunk))
+    whole = lax.all_to_all(spread, axes, split_axis=0, concat_axis=0, tiled=True)
+    return whole.reshape(-1)[:size]
+
+
 def local(
     token_ids,
     input_table,
@@ -236,7 +250,7 @@
         d_norm,
     )
     packed = jnp.concatenate([part.reshape(-1) for part in parts_list])
-    packed = lax.psum(packed, ("seq", "batch"))
+    packed = spread_sum(packed, ("seq", "batch"))
     sums = []
     offset = 0
     for part in parts_list:

time: 687 us -> 480 us (0.70)
  waiting for transfers between devices: 398 us -> 149 us
  blocking collectives: 0 us -> 62.1 us
  between operations: 15.2 us -> 1.65 us
  local copies, waits for them, and re-layouts: 103 us -> 94.8 us
    psum x1 -> x0, waiting for transfers between devices: 249 us -> none  [local(): packed = lax.psum(packed, ('seq', 'batch'))]
    all_to_all x0 -> x2, blocking collectives: none -> 62.1 us  [the longest x1 32.5 us: spread_sum(): lax.all_to_all(padded, axes, split_axis=0, concat_axis=0, tiled=True)]
  transfers between devices with their start and end apart: 7 -> 6, of which waited for: 5 -> 4; matrix products, arithmetic and copies ran while one was open for 8% -> 12% of each run, Pallas kernels for 0% -> 0%
where the time goes in v2:
time: 480 us; the launch traced here: 472 us
  waiting for transfers between devices  149 us (31%)
  local copies, waits for them, and re-layouts  94.8 us (20%)
  blocking collectives  62.1 us (13%)
  starting transfers between devices  56.8 us (12%)
  matrix products  53.7 us (11%)
  other arithmetic  53.3 us (11%)
    all_to_all x1, waiting for transfers between devices, settle_forward(): lax.all_to_all(settled, 'seq', split_axis=1, concat_axis=1, tiled=True)  45 us
    all_to_all x1, waiting for transfers between devices, local(): lax.all_to_all(flat.reshape(heads, parts, span), 'seq', split_axis=1, con...  45 us
    all_to_all x1, waiting for transfers between devices, local(): lax.all_to_all(back_flat.reshape(heads, parts, span), 'seq', split_axis=1...  43.7 us
    all_to_all x1, blocking collectives, spread_sum(): lax.all_to_all(padded, axes, split_axis=0, concat_axis=0, tiled=True)  32.5 us
    all_to_all x1, blocking collectives, spread_sum(): lax.all_to_all(spread, axes, split_axis=0, concat_axis=0, tiled=True)  29.6 us
    reshape x3, local copies, waits for them, and re-layouts, mixer_output(): gated = mixed.reshape(tokens, heads * head) * jax.nn.silu(gate_rows)  21.3 us
    dot_general x3, matrix products, mixer_output(): jnp.einsum('chts,cshp->cthp', mixing, blocked, preferred_element_type=jnp...  18.4 us
    all_to_all x1, starting transfers between devices, local(): lax.all_to_all(back_flat.reshape(heads, parts, span), 'seq', split_axis=1...  16.6 us
  transfers between devices with their start and end apart: 6, of which 4 were waited for; matrix products, arithmetic and copies ran while one was open for 12% of the time, Pallas kernels for 0%

profile of v2, /device:TPU:1, one launch (start us, length us, event | category | flops | bytes accessed | tf_op | source)
XLA Modules:
  0.0 471.7 jit_solution(14639685275968517726)
XLA Ops:
  1.4 4.9 %collective-permute-start = (s32[3]{0:T(128)S(1)}, s32[3]{0:T(128)S(1)}, u32[]{:S(2)}, u32[]{:S(2)}) collective-permute-start(s32[3]{0:T(128)S(1)} %add_bitcast_fusion), channel_id=1, source_target_pairs={{0,4},{4,8},{8,12},{12,16},{16,20},{20,24},{24,28},{28,32},{32,36}... | collective-permute-start | bytes 44 | tf_op jit(solution)/shard_map/ppermute | solution.py:18
  9.9 3.9 multiply_convert_fusion.1
  17.7 12.3 %all-to-all-start = ((f32[56,64,1]{0,2,1:T(1,128)}), f32[56,64,1]{0,2,1:T(1,128)S(1)}, u32[]{:S(2)}, u32[]{:S(2)}) async-start(f32[56,64,1]{0,2,1:T(1,128)} %broadcast_in_dim.136), calls=%async_computation | async-start | bytes 65536 | tf_op jit(solution)/shard_map/all_to_all | solution.py:196
  30.7 5.6 %reshape.328 = bf16[2,128,56,64]{3,2,1,0:T(8,128)(2,1)} reshape(bf16[256,3584]{1,0:T(8,128)(2,1)} %slice.107) | data formatting | bytes 3670016 | tf_op jit(solution)/shard_map/jvp()/reshape;jvp()/reshape | solution.py:97
  36.3 6.4 %copy.262 = bf16[2,128,56,64]{1,3,2,0:T(8,128)(2,1)} copy(bf16[2,128,56,64]{3,2,1,0:T(8,128)(2,1)} %reshape.328) | data formatting | bytes 3670016 | tf_op jit(solution)/shard_map/jvp()/reshape;jvp()/reshape | solution.py:97
  42.7 3.9 fusion.81
  46.6 6.2 %while.38 = (s32[]{:T(128)}, f32[56,64,128]{2,1,0:T(8,128)S(1)}, f32[2,56,64,128]{3,2,1,0:T(8,128)}, f32[2,56]{1,0:T(2,128)S(1)}, f32[2,56,1,1]{1,3,2,0:T(1,128)...) while((s32[]{:T(128)}, f32[56,64,128]{2,1,0:T(8,128)S(1)}, ...), condition=%wide.region_3.4_spmd.clone.clone, body=%wide.region_2.3_spmd.clone.sunk.clone | while | flops 1835011 | bytes 23857452 | solution.py:63
  52.9 2.3 copy.271
  55.1 10.8 %all-to-all-start.1 = ((f32[56,64,128]{2,0,1:T(8,128)}), f32[56,64,128]{2,0,1:T(8,128)S(1)}, u32[]{:S(2)}, u32[]{:S(2)}) async-start(f32[56,64,128]{2,0,1:T(8,128)} %copy.271), calls=%async_computation.1 | async-start | bytes 3670016 | tf_op jit(solution)/shard_map/all_to_all | solution.py:193
  66.3 45.0 %all-to-all-done.1 = f32[56,64,128]{2,0,1:T(8,128)S(1)} async-done(((f32[56,64,128]{2,0,1:T(8,128)}), f32[56,64,128]{2,0,1:T(8,128)S(1)}, u32[]{:S(2)}, u32[]{:S(2)}) %all-to-all-start.1) | async-done | bytes 1835040 | tf_op jit(solution)/shard_map/all_to_all | solution.py:193
  111.3 2.4 fusion.60
  113.7 2.3 copy.273
  116.0 6.0 %all-to-all-start.2 = ((f32[56,64,128]{2,0,1:T(8,128)}), f32[56,64,128]{2,0,1:T(8,128)S(1)}, u32[]{:S(2)}, u32[]{:S(2)}) async-start(f32[56,64,128]{2,0,1:T(8,128)} %copy.273), calls=%async_computation.2 | async-start | bytes 3670016 | tf_op jit(solution)/shard_map/all_to_all | solution.py:127
  122.3 45.0 %all-to-all-done.2 = f32[56,64,128]{2,0,1:T(8,128)S(1)} async-done(((f32[56,64,128]{2,0,1:T(8,128)}), f32[56,64,128]{2,0,1:T(8,128)S(1)}, u32[]{:S(2)}, u32[]{:S(2)}) %all-to-all-start.2) | async-done | bytes 1835040 | tf_op jit(solution)/shard_map/all_to_all | solution.py:127
  167.7 3.0 copy-done.6
  174.9 5.5 %fusion.31 = f32[2,128,56,64]{1,3,2,0:T(8,128)} fusion(bf16[2,128,56,64]{1,3,2,0:T(8,128)(2,1)S(1)} %copy-done.11, f32[2,128,56,64]{1,3,2,0:T(8,128)S(1)} %fusion.153, f32[2,56,128]{2,1,0:T(8,128)S(1)} %copy.261, f32[2,56,128]{2,1,0:T(8,128)S(1)} %copy.259, f32[2,128,128]{2,1,0:T(8,128)S(1)} %fusion.152, pred[128,128]{1,0:T(8,128)(4,1)S(1)} %iota_compare_fusion.3, ...), kind=kOutput, calls=%fused_computation.60 | convolution fusion | flops 250478592 | bytes 9494752 | tf_op jit(solution)/shard_map/jvp(chts,cshp->cthp)/dot_general | solution.py:98
  180.4 8.9 %copy.313 = f32[2,128,56,64]{3,2,1,0:T(8,128)} copy(f32[2,128,56,64]{1,3,2,0:T(8,128)} %fusion.31) | data formatting | bytes 7340032 | tf_op jit(solution)/shard_map/jvp()/reshape | solution.py:103
  189.3 6.9 %reshape.329 = f32[256,3584]{1,0:T(8,128)} reshape(f32[2,128,56,64]{3,2,1,0:T(8,128)} %copy.313) | data formatting | bytes 7340032 | tf_op jit(solution)/shard_map/jvp()/reshape | solution.py:103
  196.2 3.5 multiply_reduce_fusion.8
  202.8 3.9 multiply_reduce_fusion.4
  206.7 5.1 %copy.277 = f32[256,3584]{0,1:T(8,128)} copy(f32[256,3584]{1,0:T(8,128)} %get-tuple-element.365) | data formatting | bytes 7340032 | tf_op jit(solution)/shard_map/transpose(jvp())/mul | solution.py:103
  211.8 5.5 %reshape.307 = f32[2,128,56,64]{1,0,3,2:T(2,128)} reshape(f32[256,3584]{0,1:T(8,128)} %copy.277) | data formatting | bytes 7340032 | tf_op jit(solution)/shard_map/transpose(jvp())/reshape | solution.py:103
  217.4 4.6 multiply_reduce_fusion.5
  221.9 2.3 copy.282
  224.2 16.6 %all-to-all-start.3 = ((f32[56,64,128]{2,0,1:T(8,128)}), f32[56,64,128]{2,0,1:T(8,128)S(1)}, u32[]{:S(2)}, u32[]{:S(2)}) async-start(f32[56,64,128]{2,0,1:T(8,128)} %copy.282), calls=%async_computation.3 | async-start | bytes 3670016 | tf_op jit(solution)/shard_map/all_to_all | solution.py:218
  242.6 43.7 %all-to-all-done.3 = f32[56,64,128]{2,0,1:T(8,128)S(1)} async-done(((f32[56,64,128]{2,0,1:T(8,128)}), f32[56,64,128]{2,0,1:T(8,128)S(1)}, u32[]{:S(2)}, u32[]{:S(2)}) %all-to-all-start.3) | async-done | bytes 1835040 | tf_op jit(solution)/shard_map/all_to_all | solution.py:218
  286.3 2.4 fusion.58
  288.7 2.4 copy.284
  291.1 6.2 %all-to-all-start.4 = ((f32[56,64,128]{2,0,1:T(8,128)}), f32[56,64,128]{2,0,1:T(8,128)}, u32[]{:S(2)}, u32[]{:S(2)}) async-start(f32[56,64,128]{2,0,1:T(8,128)} %copy.284), calls=%async_computation.4 | async-start | bytes 3670016 | tf_op jit(solution)/shard_map/all_to_all | solution.py:134
  297.3 6.6 %fusion.35 = f32[16,3584]{1,0:T(8,128)S(1)} fusion(f32[256,3584]{1,0:T(8,128)} %copy-done.22, f32[256,3584]{1,0:T(8,128)} %reshape.329, f32[256,3584]{1,0:T(8,128)} %copy-done.18, bf16[1,256,3584]{2,1,0:T(8,128)(2,1)} %param.23, f32[256]{0:T(256)S(1)} %multiply_multiply_fusion.1, f32[3584]{0:T(1024)S(1)} %copy-done.23, f32[256]{0:T(256)S(1)} %fusion.135, ...), kind=kOutput, calls=%fused_computation.64 | convolution fusion | flops 190840832 | bytes 13125632 | tf_op jit(solution)/shard_map/dot_general | solution.py:244
  304.7 8.6 %fusion.14 = (f32[2,56,128]{2,1,0:T(8,128)S(1)}, f32[2,56,128]{2,1,0:T(8,128)S(1)}, f32[2,56,128]{2,1,0:T(8,128)S(1)}, bf16[2,128,128]{2,1,0:T(8,128)(2,1)S(1)}) fusion(f32[2,56,128]{2,1,0:T(8,128)S(1)} %copy.261, f32[2,56,128]{2,1,0:T(8,128)S(1)} %copy.259, f32[2,128,128]{2,1,0:T(8,128)S(1)} %fusion.152, pred[128,128]{1,0:T(8,128)(4,1)S(1)} %iota_compare_fusion.3, ...), kind=kOutput, calls=%fused_computation.28 | convolution fusion | flops 264165376 | bytes 6004736 | tf_op jit(solution)/shard_map/transpose(jvp(chts,cshp->cthp))/dot_general | solution.py:98
  313.6 3.9 multiply_reduce_fusion.6
  317.7 3.9 convert_element_type.101
  324.0 2.9 fusion.95
  326.9 15.7 %all-to-all-done.4 = f32[56,64,128]{2,0,1:T(8,128)} async-done(((f32[56,64,128]{2,0,1:T(8,128)}), f32[56,64,128]{2,0,1:T(8,128)}, u32[]{:S(2)}, u32[]{:S(2)}) %all-to-all-start.4) | async-done | bytes 1835040 | tf_op jit(solution)/shard_map/all_to_all | solution.py:134
  344.5 9.6 %while.37 = (s32[]{:T(128)}, f32[56,64,128]{2,1,0:T(8,128)S(1)}, bf16[2,56,64,128]{3,2,1,0:T(8,128)(2,1)}, f32[2,56]{1,0:T(2,128)S(1)}, f32[2,56,64,128]{3,2,1,0...) while((s32[]{:T(128)}, f32[56,64,128]{2,1,0:T(8,128)S(1)}, ...), condition=%wide.region_13.14_spmd.clone, body=%wide.region_11.13_spmd.sunk.clone | while | flops 1835011 | bytes 25692272 | solution.py:63
  346.8 2.3 fusion.181
  351.6 2.3 fusion.181
  354.0 3.0 fusion.92
  360.9 4.4 fusion.57
  368.4 6.7 %copy.308 = bf16[2,128,56,64]{3,2,1,0:T(8,128)(2,1)} copy(bf16[2,128,56,64]{1,3,2,0:T(8,128)(2,1)S(1)} %fusion.57) | data formatting | bytes 3670016 | tf_op jit(solution)/shard_map/transpose(jvp())/convert_element_type | solution.py:33
  375.1 4.8 %reshape.327 = bf16[256,3584]{1,0:T(8,128)(2,1)S(1)} reshape(bf16[2,128,56,64]{3,2,1,0:T(8,128)(2,1)} %copy.308) | data formatting | bytes 3670016 | tf_op jit(solution)/shard_map/transpose(jvp())/convert_element_type | solution.py:33
  379.8 10.4 %multiply_reduce_fusion.3 = (f32[3840]{0:T(1024)S(1)}, f32[3840]{0:T(1024)S(1)}, f32[3840]{0:T(1024)S(1)}, f32[3840]{0:T(1024)S(1)}, f32[3840]{0:T(1024)S(1)}, /*index=5*/f32[256,3840]{1,0:T(8,128)}) fusion(f32[259,3840]{1,0:T(8,128)} %copy-done.2, f32[256,3840]{1,0:T(8,128)} %get-tuple-element.374, bf16[256,3584]{1,0:T(8,128)(2,1)S(1)} %reshape.327, ...), kind=kLoop, calls=%fused_computation.52 | loop fusion | flops 22590720 | bytes 25635840 | tf_op jit(solution)/shard_map/transpose(jvp())/reduce_sum | solution.py:31
  390.4 3.3 broadcast_multiply_fusion
  393.8 2.7 fusion.17
  396.5 4.1 concatenate.7
  401.6 32.5 %all_to_all.43 = f32[256,1,557]{2,1,0:T(1,128)S(1)} all-to-all(f32[256,1,557]{2,1,0:T(1,128)S(1)} %all_to_all.34), channel_id=1, replica_groups=mesh['seq'=64,'batch'=4] {'seq','batch'}, dimensions={0} | all-to-all | bytes 1140736 | tf_op jit(solution)/shard_map/all_to_all | solution.py:144
  435.0 29.6 %all_to_all.42 = f32[256,1,557]{2,1,0:T(1,128)S(1)} all-to-all(f32[256,1,557]{2,1,0:T(1,128)S(1)} %broadcast_in_dim.143), channel_id=1, replica_groups=mesh['seq'=64,'batch'=4] {'seq','batch'}, dimensions={0} | all-to-all | bytes 1140736 | tf_op jit(solution)/shard_map/all_to_all | solution.py:147
  (182 shorter events, 51.1 us)
Async XLA Ops:
  0.6 8.4 %copy-start = (bf16[16,3840]{1,0:T(8,128)(2,1)S(1)}, bf16[16,3840]{1,0:T(8,128)(2,1)}, u32[]{:S(2)}) copy-start(bf16[16,3840]{1,0:T(8,128)(2,1)} %param.15) | copy-start | bytes 368644
  1.4 6.8 %collective-permute-start = (s32[3]{0:T(128)S(1)}, s32[3]{0:T(128)S(1)}, u32[]{:S(2)}, u32[]{:S(2)}) collective-permute-start(s32[3]{0:T(128)S(1)} %add_bitcast_fusion), channel_id=1, source_target_pairs={{0,4},{4,8},{8,12},{12,16},{16,20},{20,24},{24,28},{28,32},{32,36}... | collective-permute-start | bytes 44 | tf_op jit(solution)/shard_map/ppermute | solution.py:18
  7.0 9.3 %copy-start.29 = (f32[56]{0:T(128)}, f32[56]{0:T(128)S(1)}, u32[]{:S(2)}) copy-start(f32[56]{0:T(128)S(1)} %exponential_negate_fusion) | copy-start | bytes 676
  9.1 0.8 copy-start.24
  9.8 3.9 copy-start.2
  13.8 1.3 copy-start.7
  13.8 2.6 copy-start.26
  17.7 37.4 %all-to-all-start = ((f32[56,64,1]{0,2,1:T(1,128)}), f32[56,64,1]{0,2,1:T(1,128)S(1)}, u32[]{:S(2)}, u32[]{:S(2)}) async-start(f32[56,64,1]{0,2,1:T(1,128)} %broadcast_in_dim.136), calls=%async_computation | async-start | bytes 65536 | tf_op jit(solution)/shard_map/all_to_all | solution.py:196
  46.7 2.7 copy-start.4
  49.8 2.7 copy-start.4
  55.1 56.1 %all-to-all-start.1 = ((f32[56,64,128]{2,0,1:T(8,128)}), f32[56,64,128]{2,0,1:T(8,128)S(1)}, u32[]{:S(2)}, u32[]{:S(2)}) async-start(f32[56,64,128]{2,0,1:T(8,128)} %copy.271), calls=%async_computation.1 | async-start | bytes 3670016 | tf_op jit(solution)/shard_map/all_to_all | solution.py:193
  116.0 51.4 %all-to-all-start.2 = ((f32[56,64,128]{2,0,1:T(8,128)}), f32[56,64,128]{2,0,1:T(8,128)S(1)}, u32[]{:S(2)}, u32[]{:S(2)}) async-start(f32[56,64,128]{2,0,1:T(8,128)} %copy.273), calls=%async_computation.2 | async-start | bytes 3670016 | tf_op jit(solution)/shard_map/all_to_all | solution.py:127
  167.3 3.9 copy-start.9
  167.3 3.4 copy-start.6
  167.7 3.5 copy-start.14
  171.2 1.2 copy-start.16
  171.2 3.7 copy-start.11
  171.2 3.7 copy-start.27
  173.1 1.8 copy-start.19
  189.3 6.9 %copy-start.25 = (bf16[16,3584]{1,0:T(8,128)(2,1)S(1)}, bf16[16,3584]{1,0:T(8,128)(2,1)}, u32[]{:S(2)}) copy-start(bf16[16,3584]{1,0:T(8,128)(2,1)} %param.16) | copy-start | bytes 344068
  196.2 3.6 copy-start.20
  196.2 3.6 copy-start.23
  199.7 7.0 %copy-start.18 = (f32[256,3584]{1,0:T(8,128)}, f32[256,3584]{1,0:T(8,128)S(1)}, u32[]{:S(2)}) copy-start(f32[256,3584]{1,0:T(8,128)S(1)} %get-tuple-element.370) | copy-start | bytes 11010052
  199.8 7.0 %copy-start.22 = (f32[256,3584]{1,0:T(8,128)}, f32[256,3584]{1,0:T(8,128)S(1)}, u32[]{:S(2)}) copy-start(f32[256,3584]{1,0:T(8,128)S(1)} %get-tuple-element.389) | copy-start | bytes 11010052
  199.8 3.0 copy-start.8
  211.8 5.5 %copy-start.15 = (f32[56,64,128]{2,1,0:T(8,128)S(1)}, f32[56,64,128]{2,1,0:T(8,128)}, u32[]{:S(2)}) copy-start(f32[56,64,128]{2,1,0:T(8,128)} %copy-done.14) | copy-start | bytes 5505028
  224.2 62.1 %all-to-all-start.3 = ((f32[56,64,128]{2,0,1:T(8,128)}), f32[56,64,128]{2,0,1:T(8,128)S(1)}, u32[]{:S(2)}, u32[]{:S(2)}) async-start(f32[56,64,128]{2,0,1:T(8,128)} %copy.282), calls=%async_computation.3 | async-start | bytes 3670016 | tf_op jit(solution)/shard_map/all_to_all | solution.py:218
  291.1 51.5 %all-to-all-start.4 = ((f32[56,64,128]{2,0,1:T(8,128)}), f32[56,64,128]{2,0,1:T(8,128)}, u32[]{:S(2)}, u32[]{:S(2)}) async-start(f32[56,64,128]{2,0,1:T(8,128)} %copy.284), calls=%async_computation.4 | async-start | bytes 3670016 | tf_op jit(solution)/shard_map/all_to_all | solution.py:134
  297.3 7.4 %copy-start.12 = (bf16[2,128,56,64]{1,3,2,0:T(8,128)(2,1)S(1)}, bf16[2,128,56,64]{1,3,2,0:T(8,128)(2,1)}, u32[]{:S(2)}) copy-start(bf16[2,128,56,64]{1,3,2,0:T(8,128)(2,1)} %copy.262) | copy-start | bytes 5505028
  317.5 6.5 %copy-start.17 = (bf16[2,56,64,128]{3,2,1,0:T(8,128)(2,1)S(1)}, bf16[2,56,64,128]{3,2,1,0:T(8,128)(2,1)}, u32[]{:S(2)}) copy-start(bf16[2,56,64,128]{3,2,1,0:T(8,128)(2,1)} %copy-done.16) | copy-start | bytes 5505028
  344.5 2.4 copy-start.5
  349.2 2.4 copy-start.5
  354.0 3.0 copy-start.13
  354.0 3.1 copy-start.21
  357.2 1.5 copy-start.10
  357.2 3.7 copy-start.3
  360.8 7.1 %copy-start.28 = (f32[56]{0:T(128)S(1)}, f32[56]{0:T(128)}, u32[]{:S(2)}) copy-start(f32[56]{0:T(128)} %param.18) | copy-start | bytes 676
  360.9 7.2 %copy-start.30 = (f32[56]{0:T(128)S(1)}, f32[56]{0:T(128)}, u32[]{:S(2)}) copy-start(f32[56]{0:T(128)} %copy-done.29) | copy-start | bytes 676
  401.6 69.9 %copy-start.1 = (bf16[16,3840]{1,0:T(8,128)(2,1)S(1)}, bf16[16,3840]{1,0:T(8,128)(2,1)}, u32[]{:S(2)}) copy-start(bf16[16,3840]{1,0:T(8,128)(2,1)} %param.15) | copy-start | bytes 368644
